TPU v7x, 512 devices: a whole 4x4x16 slice. The times are simulated.
512 devices in a mesh: pool: 128 (over x, z, core), tp: 4 (over y).
Axes of the slice: x: 4, y: 4, z: 16, core: 2. Of those that a mesh axis runs over, the one named last changes fastest.
Arguments:
- hidden_rows: bfloat16 [16384, 8192], P('pool', 'tp'), may hold values from -6 to 6
- kv_weight: bfloat16 [8192, 1024], P('tp', 'pool'), may hold values from -0.0625 to 0.0625
- queries: bfloat16 [16384, 4096], P('pool', 'tp'), may hold values from -5 to 5
- cache_table: bfloat16 [1024, 128, 1024], P('pool', None, 'tp'), may hold values from -5 to 5
- retrieval: int32 [128, 64], P('pool'), may hold values from 0 to 1023, as said below
- pattern: int32 [128, 2, 64], P('pool'), may hold values 0 or 1
Outputs:
- attended: bfloat16 [16384, 4096], P('pool', 'tp')
- fresh_kv: bfloat16 [16384, 1024], P('pool', 'tp')
Inputs may be any that keep to these rules, and one draw needn't show every extreme that they name: `retrieval`: each request names 64 blocks held by 64 different devices (block b is held by device b // 8); one device, drawn from the seed, holds a block named by every request.
All inputs are finite; a program needn't handle non-finite values. No bound on the sum of `pattern` on one device may be relied on, other than what follows from the above.
Results may differ from a plain program's by a relative error of at most 0.025.
Values may be sent and summed in bfloat16 or wider, within the bound.
No kernel may reach another device: no remote copies, remote signals or barrier semaphores. Data moves between devices by JAX's collectives and lax.ppermute only.
A program may use at most 192 MiB of HBM per device.

v0:
```python
import math
import jax
import jax.numpy as jnp
import numpy as np
from jax import lax
from jax.sharding import Mesh
from jax.sharding import PartitionSpec as P

HD = 128
QH = 32
KVH = 4
BLK = 128
RBLK = 64
POOL = ("px", "pz", "pc")
ID_SPLIT = 32


def rows_by_keys(left, right):
    return lax.dot_general(
        left, right, (((1,), (1,)), ((), ())), preferred_element_type=jnp.float32
    )


def merge(carry, scores, mask, vals):
    top_now, total_now, numer_now = carry
    top_new = jnp.maximum(top_now, jnp.max(jnp.where(mask, scores, -1e30), axis=1))
    weights_now = jnp.where(mask, jnp.exp(scores - top_new[:, None]), 0.0)
    factor = jnp.exp(top_now - top_new)
    total_new = total_now * factor + jnp.sum(weights_now, axis=1)
    numer_new = numer_now * factor[:, None] + jnp.dot(
        weights_now.astype(jnp.bfloat16), vals, preferred_element_type=jnp.float32
    )
    return (top_new, total_new, numer_new)


def body(hidden_rows, kv_weight, queries, cache_table, retrieval, pattern):
    blocks_dev, blk, width = cache_table.shape
    npool = lax.axis_size(POOL)
    fetch_count = retrieval.shape[1]
    wanted = retrieval[0]
    id_row = jnp.concatenate(
        [
            (wanted // ID_SPLIT).astype(jnp.bfloat16),
            (wanted % ID_SPLIT).astype(jnp.bfloat16),
            jnp.zeros((width - 2 * fetch_count,), jnp.bfloat16),
        ]
    )
    id_block = jnp.broadcast_to(id_row[None, None, :], (1, blk, width))
    outgoing = jnp.concatenate([cache_table, id_block], axis=0)
    nx, nz, nc = (lax.axis_size(a) for a in POOL)
    rows_out = blocks_dev + 1
    step = outgoing.reshape(rows_out, nx, nz, nc, width).transpose(0, 1, 3, 2, 4)
    step = step.reshape(rows_out, nx * nc, nz, width)
    step = lax.all_to_all(step, ("px", "pc"), split_axis=1, concat_axis=1, tiled=True)
    step = lax.all_to_all(step, "pz", split_axis=2, concat_axis=2, tiled=True)
    step = step.reshape(rows_out, nx, nc, nz, width).transpose(1, 3, 2, 0, 4)
    by_token = step.reshape(npool, rows_out, width)
    table = by_token[:, :blocks_dev].reshape(npool * blocks_dev, width)
    id_rows = by_token[:, blocks_dev].astype(jnp.float32)
    wanted_all = (
        id_rows[:, :fetch_count] * ID_SPLIT + id_rows[:, fetch_count : 2 * fetch_count]
    ).astype(jnp.int32)
    picks = (
        wanted_all.reshape(-1)[:, None] == jnp.arange(npool * blocks_dev, dtype=jnp.int32)[None, :]
    ).astype(jnp.bfloat16)
    reply = jnp.dot(picks, table, preferred_element_type=jnp.float32).astype(jnp.bfloat16)
    reply = reply.reshape(npool, fetch_count, 1, width)
    reply, hidden_rows, kv_weight = lax.optimization_barrier((reply, hidden_rows, kv_weight))
    fetched = lax.all_to_all(reply, POOL, split_axis=0, concat_axis=0, tiled=True)
    w_head = lax.all_gather(kv_weight, ("pz", "pc"), axis=1, tiled=True)
    w_all = lax.all_gather(w_head, "px", axis=1, tiled=True)
    partial_kv = jnp.dot(hidden_rows, w_all, preferred_element_type=jnp.float32)
    fresh = lax.psum_scatter(partial_kv.astype(jnp.bfloat16), "tp", scatter_dimension=1, tiled=True)
    count = hidden_rows.shape[0]
    group = QH // KVH
    scale = float(HD) ** (-0.5)
    local_heads = fresh.shape[1] // (2 * HD)
    tokens_step = BLK // math.gcd(BLK, 4)
    steps_count = BLK // tokens_step
    grouped = fetched.reshape(steps_count, tokens_step * fetch_count, width)
    token_of_row = jnp.arange(count * group) // group
    block_of_row = token_of_row // RBLK
    row_pat = jnp.take(pattern[0] != 0, block_of_row, axis=0)
    mask = jnp.tile(row_pat, (1, tokens_step))
    near_mask = token_of_row[:, None] >= jnp.arange(count)[None, :]
    q_heads = queries.reshape(count, local_heads, group * HD)
    q_rows = q_heads[:, 0].reshape(count * group, HD)
    near_keys = fresh[:, 0:HD]
    near_vals = fresh[:, HD : 2 * HD]
    near_scores = rows_by_keys(q_rows, near_keys) * scale
    top = jnp.max(jnp.where(near_mask, near_scores, -1e30), axis=1)
    weights = jnp.where(near_mask, jnp.exp(near_scores - top[:, None]), 0.0)
    total = jnp.sum(weights, axis=1)
    numer = jnp.dot(weights.astype(jnp.bfloat16), near_vals, preferred_element_type=jnp.float32)

    def visit(carry, block_rows):
        keys = block_rows[:, 0:HD]
        vals = block_rows[:, HD : 2 * HD]
        scores = rows_by_keys(q_rows, keys) * scale
        return (merge(carry, scores, mask, vals), None)

    (top, total, numer), unused = lax.scan(visit, (top, total, numer), grouped)
    results = (numer / total[:, None]).reshape(count, group * HD)
    attended = results.astype(jnp.bfloat16)
    return (attended, fresh)


def solution(mesh):
    npool = mesh.shape["pool"]
    ntp = mesh.shape["tp"]
    nx = 4 if npool % 8 == 0 else 1
    fine = Mesh(
        np.asarray(mesh.devices).reshape(nx, npool // (2 * nx), 2, ntp), ("px", "pz", "pc", "tp")
    )
    placed = (
        P(POOL, "tp"),
        P("tp", POOL),
        P(POOL, "tp"),
        P(POOL, None, "tp"),
        P(POOL, None),
        P(POOL, None, None),
    )
    return jax.shard_map(
        body, mesh=fine, in_specs=placed, out_specs=(P(POOL, "tp"), P(POOL, "tp")), check_vma=False
    )
```

profile of v0, /device:TPU:34, one launch (start us, length us, event | category | flops | bytes accessed | tf_op | source)
XLA Modules:
  0.0 318.3 jit_solution(7537971316295151175)
XLA Ops:
  7.2 0.7 fusion.32
  7.9 0.1 pad_maximum_fusion.1
  8.0 1.1 pad_maximum_fusion
  9.1 0.2 reshape.149
  9.3 0.1 copy.22
  9.4 14.3 %all_to_all.15 = bf16[9,8,16,256]{3,2,0,1:T(8,128)(2,1)S(1)} all-to-all(bf16[9,8,16,256]{3,2,0,1:T(8,128)(2,1)S(1)} %bitcast.88), channel_id=1, replica_groups=mesh['px'=4,'pz'=16,'pc'=2,'tp'=4] {'px','pc'}, dimensions={1} | all-to-all | bytes 1179648 | tf_op jit(solution)/shard_map/all_to_all | solution.py:54
  23.7 0.2 copy.17
  23.9 49.4 %all_to_all.16 = bf16[9,8,16,256]{3,1,0,2:T(8,128)(2,1)S(1)} all-to-all(bf16[9,8,16,256]{3,1,0,2:T(8,128)(2,1)S(1)} %copy.17), channel_id=1, replica_groups=mesh['px'=4,'pz'=16,'pc'=2,'tp'=4] {'pz'}, dimensions={2} | all-to-all | bytes 1179648 | tf_op jit(solution)/shard_map/all_to_all | solution.py:55
  73.3 0.2 reshape.151
  73.5 0.6 copy.28
  74.1 0.2 reshape.152
  74.4 0.1 fusion.22
  74.5 0.1 eq.17
  74.6 9.2 %fusion.11 = bf16[8192,256]{1,0:T(8,128)(2,1)} fusion(s32[8192]{0:T(1024)S(1)} %eq.17, bf16[128,8,256]{2,0,1:T(8,128)(2,1)S(1)} %slice.39), kind=kOutput, calls=%fused_computation.19 | convolution fusion | flops 4305453056 | bytes 4751360 | tf_op jit(solution)/shard_map/dot_general | solution.py:66
  83.8 8.1 %all-to-all-start.2 = ((bf16[128,64,1,256]{3,1,2,0:T(8,128)(2,1)}), bf16[128,64,1,256]{3,1,2,0:T(8,128)(2,1)}, u32[]{:S(2)}, u32[]{:S(2)}) async-start(bf16[128,64,1,256]{3,1,2,0:T(8,128)(2,1)} %bitcast.86), calls=%async_computation.3 | async-start | bytes 8388608 | tf_op jit(solution)/shard_map/all_to_all | solution.py:69
  91.9 0.7 all-gather.3.cloned.1.call-update
  92.6 91.3 %all-gather.3.cloned.1.call-done = bf16[2048,256]{0,1:T(8,128)(2,1)} async-done(((bf16[2048,8]{0,1:T(8,128)(2,1)}), bf16[2048,256]{0,1:T(8,128)(2,1)}) %all-gather.3.cloned.1.call-update) | async-done | bytes 1048592 | tf_op jit(solution)/shard_map/all_gather | solution.py:70
  184.0 0.2 reduce-scatter.2.cloned.1.call-start
  184.2 66.6 %all-gather.5.cloned.1.call-done = bf16[2048,1024]{0,1:T(8,128)(2,1)} async-done(((bf16[2048,256]{0,1:T(8,128)(2,1)}), bf16[2048,1024]{0,1:T(8,128)(2,1)}) %all-gather.5.cloned.1.call-update) | async-done | bytes 4194320 | tf_op jit(solution)/shard_map/all_gather | solution.py:71
  250.8 4.4 %convolution_convert_fusion = bf16[128,1024]{1,0:T(8,128)(2,1)} fusion(bf16[128,2048]{1,0:T(8,128)(2,1)S(1)} %copy-done, bf16[2048,1024]{0,1:T(8,128)(2,1)} %all-gather.5.cloned.1.call-done), kind=kOutput, calls=%fused_computation.22 | convolution fusion | flops 537001984 | bytes 4980736 | tf_op jit(solution)/shard_map/dot_general | solution.py:72
  255.3 3.0 gather_fusion
  258.3 0.2 broadcast_select_fusion
  258.5 0.2 copy.21
  258.7 0.1 reshape_squeeze_reshape.3
  258.9 24.5 %reduce-scatter.2.cloned.1.call-done = bf16[128,256]{1,0:T(8,128)(2,1)} async-done(((bf16[128,1024]{1,0:T(8,128)(2,1)}), bf16[128,256]{1,0:T(8,128)(2,1)}) %reduce-scatter.2.cloned.1.call-update) | async-done | bytes 65552 | tf_op jit(solution)/shard_map/reduce_scatter | solution.py:73
  283.3 1.0 select_reduce_fusion
  284.3 0.1 fusion.16
  284.5 1.0 fusion.17
  285.5 0.6 all-to-all-done.2
  286.1 24.6 %while.15 = (s32[]{:T(128)}, f32[1024]{0:T(1024)S(1)}, f32[1024]{0:T(1024)S(1)}, f32[1024,128]{1,0:T(8,128)S(1)}, bf16[4,2048,256]{2,1,0:T(8,128)(2,1)}, /*index...) while((s32[]{:T(128)}, f32[1024]{0:T(1024)S(1)}, f32[1024]{0:T(1024)S(1)}, ...), condition=%wide.region_6.7_spmd.clone, body=%wide.region_3.6_spmd.clone.sunk | while | flops 1090783232 | bytes 29814880 | solution.py:102
  286.1 1.3 dynamic-slice_bitcast_fusion.2
  287.4 1.3 fusion.47
  288.7 1.9 fusion.48
  290.7 1.5 convolution_add_fusion.2
  292.3 1.3 dynamic-slice_bitcast_fusion.2
  293.6 1.3 fusion.47
  294.9 1.9 fusion.48
  296.9 1.5 convolution_add_fusion.2
  298.4 1.3 dynamic-slice_bitcast_fusion.2
  299.7 1.3 fusion.47
  301.1 1.9 fusion.48
  303.0 1.5 convolution_add_fusion.2
  304.6 1.3 dynamic-slice_bitcast_fusion.2
  305.9 1.3 fusion.47
  307.2 1.9 fusion.48
  309.2 1.5 convolution_add_fusion.2
  310.7 0.2 divide_convert_fusion
  311.0 0.8 convert_element_type.43
  (31 shorter events, 0.3 us)
Async XLA Ops:
  7.2 243.6 %copy-start = (bf16[128,2048]{1,0:T(8,128)(2,1)S(1)}, bf16[128,2048]{1,0:T(8,128)(2,1)}, u32[]{:S(2)}) copy-start(bf16[128,2048]{1,0:T(8,128)(2,1)} %param.8) | copy-start | bytes 1572868
  83.8 171.5 %copy-start.2 = (s32[1,2,64]{2,1,0:T(2,128)S(1)}, s32[1,2,64]{2,1,0:T(2,128)}, u32[]{:S(2)}) copy-start(s32[1,2,64]{2,1,0:T(2,128)} %param.13) | copy-start | bytes 1540
  83.8 175.0 %copy-start.1 = (bf16[128,1024]{1,0:T(8,128)(2,1)S(1)}, bf16[128,1024]{1,0:T(8,128)(2,1)}, u32[]{:S(2)}) copy-start(bf16[128,1024]{1,0:T(8,128)(2,1)} %param.10) | copy-start | bytes 786436
  83.8 202.4 %all-to-all-start.2 = ((bf16[128,64,1,256]{3,1,2,0:T(8,128)(2,1)}), bf16[128,64,1,256]{3,1,2,0:T(8,128)(2,1)}, u32[]{:S(2)}, u32[]{:S(2)}) async-start(bf16[128,64,1,256]{3,1,2,0:T(8,128)(2,1)} %bitcast.86), calls=%async_computation.3 | async-start | bytes 8388608 | tf_op jit(solution)/shard_map/all_to_all | solution.py:69
  91.9 92.1 %all-gather.3.cloned.1.call-start = ((), (), s32[]{:S(2)}) async-start(), calls=%async_computation.4 | async-start | bytes 1081344 | tf_op jit(solution)/shard_map/all_gather | solution.py:70
  92.6 158.2 %all-gather.5.cloned.1.call-start = ((), (), s32[]{:S(2)}) async-start(), calls=%async_computation.5 | async-start | bytes 5242880 | tf_op jit(solution)/shard_map/all_gather | solution.py:71
  184.0 99.4 %reduce-scatter.2.cloned.1.call-start = ((), (), s32[]{:S(2)}) async-start(), calls=%async_computation.6 | async-start | bytes 327680 | tf_op jit(solution)/shard_map/reduce_scatter | solution.py:73
Sparse Core Ops, SparseCore 0:
  94.8 89.0 all-gather.2
  186.0 64.7 all-gather.4
  255.4 27.9 reduce-scatter.1
where the time goes:
time: 319 us; the launch traced here: 318 us
  waiting for transfers between devices  184 us (58%)
  blocking collectives  63.7 us (20%)
  matrix products  27 us (8%)
  between operations  13.9 us (4%)
  local copies, waits for them, and re-layouts  11 us (3%)
  other arithmetic  10.4 us (3%)
  starting transfers between devices  8.39 us (3%)
    all_gather x1, waiting for transfers between devices, body(): w_head = lax.all_gather(kv_weight, ('pz', 'pc'), axis=1, tiled=True)  91.3 us
    all_gather x1, waiting for transfers between devices, body(): w_all = lax.all_gather(w_head, 'px', axis=1, tiled=True)  66.6 us
    all_to_all x1, blocking collectives, body(): step = lax.all_to_all(step, 'pz', split_axis=2, concat_axis=2, tiled=True)  49.4 us
    reduce_scatter x1, waiting for transfers between devices, body(): lax.psum_scatter(partial_kv.astype(jnp.bfloat16), 'tp', scatter_dimension...  24.5 us
    all_to_all x1, blocking collectives, body(): lax.all_to_all(step, ('px', 'pc'), split_axis=1, concat_axis=1, tiled=True)  14.3 us
    dot_general x1, matrix products, body(): jnp.dot(picks, table, preferred_element_type=jnp.float32)  9.18 us
    all_to_all x1, starting transfers between devices, body(): lax.all_to_all(reply, POOL, split_axis=0, concat_axis=0, tiled=True)  8.1 us
    convert_element_type x4, other arithmetic, merge(): weights_now.astype(jnp.bfloat16)  7.79 us
  transfers between devices with their start and end apart: 4, of which 4 were waited for; matrix products, arithmetic and copies ran while one was open for 3% of the time, Pallas kernels for 0%

commit v1 on v0

--- a/solution.py
+++ b/solution.py
@@ -52,7 +52,9 @@
     step = outgoing.reshape(rows_out, nx, nz, nc, width).transpose(0, 1, 3, 2, 4)
     step = step.reshape(rows_out, nx * nc, nz, width)
     step = lax.all_to_all(step, ("px", "pc"), split_axis=1, concat_axis=1, tiled=True)
-    step = lax.all_to_all(step, "pz", split_axis=2, concat_axis=2, tiled=True)
+    step = jnp.concatenate(
+        lax.all_to_all(jnp.stack(jnp.split(step, lax.axis_size("pz"), axis=2)), "pz", 0, 0), axis=2
+    )
     step = step.reshape(rows_out, nx, nc, nz, width).transpose(1, 3, 2, 0, 4)
     by_token = step.reshape(npool, rows_out, width)
     table = by_token[:, :blocks_dev].reshape(npool * blocks_dev, width)

time: 319 us -> 320 us (level)
  the two profiles are of different devices: /device:TPU:34 before, /device:TPU:58 now
where the time goes in v1:
time: 320 us; the launch traced here: 319 us
  waiting for transfers between devices  184 us (58%)
  blocking collectives  63.7 us (20%)
  matrix products  27 us (8%)
  between operations  14.1 us (4%)
  local copies, waits for them, and re-layouts  12 us (4%)
  other arithmetic  10.4 us (3%)
  starting transfers between devices  8.4 us (3%)
    all_gather x1, waiting for transfers between devices, body(): w_head = lax.all_gather(kv_weight, ('pz', 'pc'), axis=1, tiled=True)  92.3 us
    all_gather x1, waiting for transfers between devices, body(): w_all = lax.all_gather(w_head, 'px', axis=1, tiled=True)  65.3 us
    all_to_all x1, blocking collectives, body(): lax.all_to_all(jnp.stack(jnp.split(step, lax.axis_size('pz'), axis=2)), '...  49.4 us
    reduce_scatter x1, waiting for transfers between devices, body(): lax.psum_scatter(partial_kv.astype(jnp.bfloat16), 'tp', scatter_dimension...  22.6 us
    all_to_all x1, blocking collectives, body(): lax.all_to_all(step, ('px', 'pc'), split_axis=1, concat_axis=1, tiled=True)  14.3 us
    dot_general x1, matrix products, body(): jnp.dot(picks, table, preferred_element_type=jnp.float32)  9.18 us
    all_to_all x1, starting transfers between devices, body(): lax.all_to_all(reply, POOL, split_axis=0, concat_axis=0, tiled=True)  8.1 us
    convert_element_type x4, other arithmetic, merge(): weights_now.astype(jnp.bfloat16)  7.79 us
  transfers between devices with their start and end apart: 4, of which 4 were waited for; matrix products, arithmetic and copies ran while one was open for 3% of the time, Pallas kernels for 0%

profile of v1, /device:TPU:58, one launch (start us, length us, event | category | flops | bytes accessed | tf_op | source)
XLA Modules:
  0.0 319.3 jit_solution(3861573533596990268)
XLA Ops:
  7.2 0.7 fusion.48
  7.9 0.1 pad_maximum_fusion.1
  8.0 1.1 pad_maximum_fusion
  9.1 0.2 reshape.149
  9.3 0.1 copy.213
  9.4 14.3 %all_to_all.15 = bf16[9,8,16,256]{3,2,0,1:T(8,128)(2,1)S(1)} all-to-all(bf16[9,8,16,256]{3,2,0,1:T(8,128)(2,1)S(1)} %bitcast.153), channel_id=1, replica_groups=mesh['px'=4,'pz'=16,'pc'=2,'tp'=4] {'px','pc'}, dimensions={1} | all-to-all | bytes 1179648 | tf_op jit(solution)/shard_map/all_to_all | solution.py:54
  23.7 0.9 fusion.50
  24.9 49.4 %all_to_all.16 = bf16[16,9,8,1,256]{4,2,1,3,0:T(8,128)(2,1)S(1)} all-to-all(bf16[16,9,8,1,256]{4,2,1,3,0:T(8,128)(2,1)S(1)} %fusion.24), channel_id=1, replica_groups=mesh['px'=4,'pz'=16,'pc'=2,'tp'=4] {'pz'}, dimensions={0} | all-to-all | bytes 1179648 | tf_op jit(solution)/shard_map/all_to_all | solution.py:56
  74.3 0.2 reshape_reshape.3
  74.5 0.6 copy.283
  75.2 0.2 reshape.152
  75.5 0.1 fusion.22
  75.5 0.1 eq.17
  75.6 9.2 %fusion.11 = bf16[8192,256]{1,0:T(8,128)(2,1)} fusion(s32[8192]{0:T(1024)S(1)} %eq.17, bf16[128,8,256]{2,0,1:T(8,128)(2,1)S(1)} %slice.39), kind=kOutput, calls=%fused_computation.19 | convolution fusion | flops 4305453056 | bytes 4751360 | tf_op jit(solution)/shard_map/dot_general | solution.py:68
  84.8 8.1 %all-to-all-start.2 = ((bf16[128,64,1,256]{3,1,2,0:T(8,128)(2,1)}), bf16[128,64,1,256]{3,1,2,0:T(8,128)(2,1)}, u32[]{:S(2)}, u32[]{:S(2)}) async-start(bf16[128,64,1,256]{3,1,2,0:T(8,128)(2,1)} %bitcast.151), calls=%async_computation.3 | async-start | bytes 8388608 | tf_op jit(solution)/shard_map/all_to_all | solution.py:71
  93.0 0.7 all-gather.3.cloned.1.call-update
  93.7 92.3 %all-gather.3.cloned.1.call-done = bf16[2048,256]{0,1:T(8,128)(2,1)} async-done(((bf16[2048,8]{0,1:T(8,128)(2,1)}), bf16[2048,256]{0,1:T(8,128)(2,1)}) %all-gather.3.cloned.1.call-update) | async-done | bytes 1048592 | tf_op jit(solution)/shard_map/all_gather | solution.py:72
  186.0 0.2 reduce-scatter.2.cloned.1.call-start
  186.3 65.3 %all-gather.5.cloned.1.call-done = bf16[2048,1024]{0,1:T(8,128)(2,1)} async-done(((bf16[2048,256]{0,1:T(8,128)(2,1)}), bf16[2048,1024]{0,1:T(8,128)(2,1)}) %all-gather.5.cloned.1.call-update) | async-done | bytes 4194320 | tf_op jit(solution)/shard_map/all_gather | solution.py:73
  251.5 4.4 %convolution_convert_fusion = bf16[128,1024]{1,0:T(8,128)(2,1)} fusion(bf16[128,2048]{1,0:T(8,128)(2,1)S(1)} %copy-done, bf16[2048,1024]{0,1:T(8,128)(2,1)} %all-gather.5.cloned.1.call-done), kind=kOutput, calls=%fused_computation.22 | convolution fusion | flops 537001984 | bytes 4980736 | tf_op jit(solution)/shard_map/dot_general | solution.py:74
  256.0 3.0 gather_fusion
  259.0 0.2 broadcast_select_fusion
  259.2 0.2 copy.212
  259.5 0.1 reshape_squeeze_reshape.3
  259.6 22.6 %reduce-scatter.2.cloned.1.call-done = bf16[128,256]{1,0:T(8,128)(2,1)} async-done(((bf16[128,1024]{1,0:T(8,128)(2,1)}), bf16[128,256]{1,0:T(8,128)(2,1)}) %reduce-scatter.2.cloned.1.call-update) | async-done | bytes 65552 | tf_op jit(solution)/shard_map/reduce_scatter | solution.py:75
  282.2 1.0 select_reduce_fusion
  283.2 0.1 fusion.16
  283.3 1.0 fusion.17
  284.4 2.8 all-to-all-done.2
  287.2 24.6 %while.15 = (s32[]{:T(128)}, f32[1024]{0:T(1024)S(1)}, f32[1024]{0:T(1024)S(1)}, f32[1024,128]{1,0:T(8,128)S(1)}, bf16[4,2048,256]{2,1,0:T(8,128)(2,1)}, /*index...) while((s32[]{:T(128)}, f32[1024]{0:T(1024)S(1)}, f32[1024]{0:T(1024)S(1)}, ...), condition=%wide.region_6.7_spmd.clone, body=%wide.region_3.6_spmd.clone.sunk | while | flops 1090783232 | bytes 29814880 | solution.py:104
  287.2 1.3 dynamic-slice_bitcast_fusion.2
  288.5 1.3 fusion.64
  289.8 1.9 fusion.65
  291.8 1.5 convolution_add_fusion.2
  293.3 1.3 dynamic-slice_bitcast_fusion.2
  294.6 1.3 fusion.64
  295.9 1.9 fusion.65
  297.9 1.5 convolution_add_fusion.2
  299.5 1.3 dynamic-slice_bitcast_fusion.2
  300.8 1.3 fusion.64
  302.1 1.9 fusion.65
  304.1 1.5 convolution_add_fusion.2
  305.6 1.3 dynamic-slice_bitcast_fusion.2
  306.9 1.3 fusion.64
  308.3 1.9 fusion.65
  310.2 1.5 convolution_add_fusion.2
  311.8 0.2 divide_convert_fusion
  312.0 0.8 convert_element_type.43
  (47 shorter events, 0.5 us)
Async XLA Ops:
  7.2 244.4 %copy-start = (bf16[128,2048]{1,0:T(8,128)(2,1)S(1)}, bf16[128,2048]{1,0:T(8,128)(2,1)}, u32[]{:S(2)}) copy-start(bf16[128,2048]{1,0:T(8,128)(2,1)} %param.8) | copy-start | bytes 1572868
  84.8 171.2 %copy-start.2 = (s32[1,2,64]{2,1,0:T(2,128)S(1)}, s32[1,2,64]{2,1,0:T(2,128)}, u32[]{:S(2)}) copy-start(s32[1,2,64]{2,1,0:T(2,128)} %param.13) | copy-start | bytes 1540
  84.8 174.6 %copy-start.1 = (bf16[128,1024]{1,0:T(8,128)(2,1)S(1)}, bf16[128,1024]{1,0:T(8,128)(2,1)}, u32[]{:S(2)}) copy-start(bf16[128,1024]{1,0:T(8,128)(2,1)} %param.10) | copy-start | bytes 786436
  84.8 202.4 %all-to-all-start.2 = ((bf16[128,64,1,256]{3,1,2,0:T(8,128)(2,1)}), bf16[128,64,1,256]{3,1,2,0:T(8,128)(2,1)}, u32[]{:S(2)}, u32[]{:S(2)}) async-start(bf16[128,64,1,256]{3,1,2,0:T(8,128)(2,1)} %bitcast.151), calls=%async_computation.3 | async-start | bytes 8388608 | tf_op jit(solution)/shard_map/all_to_all | solution.py:71
  92.9 93.1 %all-gather.3.cloned.1.call-start = ((), (), s32[]{:S(2)}) async-start(), calls=%async_computation.4 | async-start | bytes 1081344 | tf_op jit(solution)/shard_map/all_gather | solution.py:72
  93.6 157.9 %all-gather.5.cloned.1.call-start = ((), (), s32[]{:S(2)}) async-start(), calls=%async_computation.5 | async-start | bytes 5242880 | tf_op jit(solution)/shard_map/all_gather | solution.py:73
  186.0 96.2 %reduce-scatter.2.cloned.1.call-start = ((), (), s32[]{:S(2)}) async-start(), calls=%async_computation.6 | async-start | bytes 327680 | tf_op jit(solution)/shard_map/reduce_scatter | solution.py:75
Sparse Core Ops, SparseCore 0:
  95.9 90.0 all-gather.2
  188.1 63.4 all-gather.4
  256.1 26.0 reduce-scatter.1
